TPU v7x, 32 devices: a whole 2x2x4 slice. The times are simulated.
32 devices in a mesh: group: 2 (over y), seq: 8 (over z, x), chan: 2 (over core).
Axes of the slice: x: 2, y: 2, z: 4, core: 2. Of those that a mesh axis runs over, the one named last changes fastest.
Arguments:
- fresh: bfloat16 [2048, 3, 2048], P(('group', 'seq'), None, 'chan'), parts along dimension 0, may hold values from -6 to 6
- library: bfloat16 [8, 8, 2048], P('seq', None, 'chan'), may hold values from -6 to 6
- block_slot: int32 [8], replicated, may hold values from 0 to 7, each once
- prefix_blocks: int32 [16, 4], P('group'), parts along dimension 0, may hold values from 0 to 7, all different within a row
- short_taps: float32 [3, 3, 2048], P(None, None, 'chan'), may hold values from -4 to 4
- long_filter: float32 [1024, 2048], P('seq', 'chan'), may hold values from -2 to 2
- skip_gain: float32 [2048], P('chan'), may hold values from -6 to 6
Outputs:
- mixed: bfloat16 [2048, 2048], P(('group', 'seq'), 'chan'), parts along dimension 0
There are 2 independent parts, one for each index of `group`. A program takes and returns all parts, laid end to end along the dimension named above; an argument that names none is the same for every part. Nothing has to cross between parts.
Inputs may be any that keep to these rules, and one draw needn't show every extreme that they name: `block_slot`: each number appears once. `prefix_blocks`: every library block is named at least once; the four entries of a row differ.
All inputs are finite; a program needn't handle non-finite values.
Results may differ from a plain program's by a relative error of at most 0.008.
Values may be sent and summed in bfloat16 or wider, within the bound.
No kernel may reach another device: no remote copies, remote signals or barrier semaphores. Data moves between devices by JAX's collectives and lax.ppermute only.
A program may use at most 64 MiB of HBM per device.

v0:
```python
import math
import jax
import jax.numpy as jnp
from jax import lax
from jax.sharding import PartitionSpec as P

TAPS = 3
BLK = 8


def from_behind(shard, axis, by):
    count = lax.axis_size(axis)
    pairs = [(i, i + by) for i in range(count) if 0 <= i + by < count]
    return lax.ppermute(shard, axis, pairs)


def exact_dot(pattern, matrix, tensor):
    return jnp.einsum(pattern, matrix, tensor, precision=lax.Precision.HIGHEST)


def turn_angles(numbers, period):
    return (numbers % period).astype(jnp.float32) * (2.0 * math.pi / period)


def body(fresh, library, block_slot, prefix_blocks, short_taps, long_filter, skip_gain):
    row_count = fresh.shape[0]
    channels = fresh.shape[2]
    devices = lax.axis_size("seq")
    seq_index = lax.axis_index("seq")
    group_rows = row_count // devices
    period = 2 * row_count * devices
    block_ids = jnp.arange(devices, dtype=jnp.int32)
    mode_ids = jnp.arange(2 * devices, dtype=jnp.int32)
    coarse = turn_angles(mode_ids[:, None] * block_ids[None, :], 2 * devices)
    cos_q = jnp.cos(coarse)
    sin_q = jnp.sin(coarse)
    local_rows = seq_index * group_rows + jnp.arange(group_rows, dtype=jnp.int32)
    twist = turn_angles(mode_ids[:, None] * local_rows[None, :], period)
    twist_cos = jnp.cos(twist)[:, :, None]
    twist_sin = jnp.sin(twist)[:, :, None]
    row_ids = jnp.arange(row_count, dtype=jnp.int32)
    fine_angles = turn_angles(row_ids[:, None] * row_ids[None, :], row_count)
    cos_m = jnp.cos(fine_angles)
    sin_m = jnp.sin(fine_angles)
    first_modes = 2 * seq_index + jnp.arange(2, dtype=jnp.int32)
    back_twist = turn_angles(first_modes[:, None] * row_ids[None, :], period)
    back_cos = jnp.cos(back_twist)[:, :, None]
    back_sin = jnp.sin(back_twist)[:, :, None]

    def to_modes(column):
        real_part = exact_dot("kq,qgc->kgc", cos_q, column)
        imag_part = -exact_dot("kq,qgc->kgc", sin_q, column)
        return jnp.stack(
            [
                real_part * twist_cos + imag_part * twist_sin,
                imag_part * twist_cos - real_part * twist_sin,
            ]
        )

    def to_spectrum(spread):
        real_part = exact_dot("ki,jic->jkc", cos_m, spread[0]) + exact_dot(
            "ki,jic->jkc", sin_m, spread[1]
        )
        imag_part = exact_dot("ki,jic->jkc", cos_m, spread[1]) - exact_dot(
            "ki,jic->jkc", sin_m, spread[0]
        )
        return (real_part, imag_part)

    blocks_here = row_count // BLK
    flat_ids = prefix_blocks.reshape(-1)
    first_block = jnp.minimum(seq_index * blocks_here, flat_ids.shape[0] - blocks_here)
    own_ids = lax.dynamic_slice_in_dim(flat_ids, first_block, blocks_here)
    matches = own_ids[:, None] == jnp.arange(block_slot.shape[0], dtype=jnp.int32)[None, :]
    wanted = jnp.sum(jnp.where(matches, block_slot[None, :], 0), axis=1)
    shards = lax.all_gather(library, "seq", axis=0, tiled=True)
    picker = (wanted[:, None] == jnp.arange(shards.shape[0], dtype=jnp.int32)[None, :]).astype(
        jnp.bfloat16
    )
    gathered = jnp.einsum("bn,nlc->blc", picker, shards, preferred_element_type=jnp.float32)
    cached = gathered.reshape(row_count, channels).astype(jnp.bfloat16)
    values = jnp.where(seq_index < devices // 4, cached, fresh[:, 2])
    stacked = jnp.concatenate([fresh[:, :2], values[:, None]], axis=1)
    previous = from_behind(stacked[row_count - (TAPS - 1) :], "seq", 1)
    extended = jnp.concatenate([previous, stacked], axis=0)
    shortened = jnp.zeros((row_count, 3, channels), jnp.float32)
    for offset in range(TAPS):
        window_start = TAPS - 1 - offset
        shortened = shortened + short_taps[offset][None] * extended[
            window_start : window_start + row_count
        ].astype(jnp.float32)
    gating = shortened[:, 0]
    signal = shortened[:, 1] * shortened[:, 2]
    spread_signal = to_modes(
        lax.all_to_all(signal[None], "seq", split_axis=1, concat_axis=0, tiled=True)
    )
    spread_taps = to_modes(
        lax.all_to_all(long_filter[None], "seq", split_axis=1, concat_axis=0, tiled=True)
    )
    moved_signal, moved_taps = (
        lax.all_to_all(
            spread_signal.astype(jnp.bfloat16), "seq", split_axis=1, concat_axis=2, tiled=True
        ).astype(spread_signal.dtype),
        lax.all_to_all(
            spread_taps.astype(jnp.bfloat16), "seq", split_axis=1, concat_axis=2, tiled=True
        ).astype(spread_taps.dtype),
    )
    sig_real, sig_imag = to_spectrum(moved_signal)
    tap_real, tap_imag = to_spectrum(moved_taps)
    prod_real = sig_real * tap_real - sig_imag * tap_imag
    prod_imag = sig_real * tap_imag + sig_imag * tap_real
    back_real = exact_dot("ki,jic->jkc", cos_m, prod_real) - exact_dot(
        "ki,jic->jkc", sin_m, prod_imag
    )
    back_imag = exact_dot("ki,jic->jkc", cos_m, prod_imag) + exact_dot(
        "ki,jic->jkc", sin_m, prod_real
    )
    turned = jnp.stack(
        [back_real * back_cos - back_imag * back_sin, back_imag * back_cos + back_real * back_sin]
    )
    spread = lax.all_to_all(turned, "seq", split_axis=2, concat_axis=1, tiled=True)
    positions = (
        exact_dot("kq,kgc->qgc", cos_q, spread[0]) - exact_dot("kq,kgc->qgc", sin_q, spread[1])
    ) / period
    convolved = lax.all_to_all(positions, "seq", split_axis=0, concat_axis=1, tiled=True)[0]
    output = gating * (convolved + skip_gain[None, :] * signal)
    return output.astype(jnp.bfloat16)


def solution(mesh):
    return jax.shard_map(
        body,
        mesh=mesh,
        in_specs=(
            P(("group", "seq"), None, "chan"),
            P("seq", None, "chan"),
            P(),
            P("group", None),
            P(None, None, "chan"),
            P("seq", "chan"),
            P("chan"),
        ),
        out_specs=P(("group", "seq"), "chan"),
        check_vma=False,
    )
```

profile of v0, /device:TPU:0, one launch (start us, length us, event | category | flops | bytes accessed | tf_op | source)
XLA Modules:
  0.0 217.2 jit_solution(2624598276856022187)
XLA Ops:
  0.0 2.3 %broadcast_in_dim.12 = f32[1,128,1024]{2,0,1:T(1,128)} reshape(f32[128,1024]{1,0:T(8,128)} %param.12) | data formatting | bytes 1048576 | tf_op jit(solution)/shard_map/broadcast_in_dim | solution.py:97
  2.3 7.3 %all-to-all-start.2 = ((f32[1,128,1024]{2,0,1:T(1,128)}), f32[1,128,1024]{2,0,1:T(1,128)S(1)}, u32[]{:S(2)}, u32[]{:S(2)}) async-start(f32[1,128,1024]{2,0,1:T(1,128)} %broadcast_in_dim.12), calls=%async_computation.2 | async-start | bytes 1048576 | tf_op jit(solution)/shard_map/all_to_all | solution.py:97
  9.8 37.2 %all_gather.3 = bf16[8,8,1024]{2,1,0:T(8,128)(2,1)S(1)} all-gather(bf16[1,8,1024]{2,1,0:T(8,128)(2,1)S(1)} %copy-done.7), channel_id=1, replica_groups=mesh['group'=2,'seq'=8,'chan'=2] {'seq'}, dimensions={0}, use_global_device_ids=true | all-gather | bytes 147456 | tf_op jit(solution)/shard_map/all_gather | solution.py:75
  47.6 1.3 collective-permute-start
  48.9 1.4 collective-permute-done
  51.1 1.4 copy.63
  52.4 5.6 %all-to-all-start = ((f32[1,128,1024]{2,0,1:T(1,128)}), f32[1,128,1024]{2,0,1:T(1,128)S(1)}, u32[]{:S(2)}, u32[]{:S(2)}) async-start(f32[1,128,1024]{2,0,1:T(1,128)} %copy.63), calls=%async_computation | async-start | bytes 1048576 | tf_op jit(solution)/shard_map/all_to_all | solution.py:94
  59.5 2.2 %fusion.15 = f32[16,16,1024]{2,0,1:T(8,128)} fusion(f32[8,16,1024]{2,1,0:T(8,128)S(1)} %bitcast.138), kind=kOutput, calls=%fused_computation.44 | convolution fusion | flops 25167616 | bytes 1572864 | tf_op jit(solution)/shard_map/kq,qgc->kgc/dot_general | solution.py:18
  61.7 6.6 %all-to-all-done = f32[1,128,1024]{2,0,1:T(1,128)S(1)} async-done(((f32[1,128,1024]{2,0,1:T(1,128)}), f32[1,128,1024]{2,0,1:T(1,128)S(1)}, u32[]{:S(2)}, u32[]{:S(2)}) %all-to-all-start) | async-done | bytes 524320 | tf_op jit(solution)/shard_map/all_to_all | solution.py:94
  69.7 2.5 %fusion.9 = (bf16[1,16,16,1024]{3,1,2,0:T(8,128)(2,1)S(1)}, bf16[1,16,16,1024]{3,1,2,0:T(8,128)(2,1)S(1)}, bf16[1,16,16,1024]{3,1,2,0:T(8,128)(2,1)S(1)}, bf16[1,16,16,1024]{3,1,2,0:T(8,128)(2,1)}) fusion(f32[16,16,1024]{2,0,1:T(8,128)S(1)} %convolution_negate_fusion, f32[16,16,1024]{2,0,1:T(8,128)S(1)} %copy-done.3, f32[16,16]{0,1:T(8,128)S(1)} %get-tuple-element.27, ...), kind=kOutput, calls=%fused_computation.35 | convolution fusion | flops 29361920 | bytes 5769216 | tf_op jit(solution)/shard_map/kq,qgc->kgc/dot_general | solution.py:18
  72.2 1.5 copy.74
  73.8 3.7 %all-to-all-start.3 = ((bf16[2,16,16,1024]{3,2,0,1:T(8,128)(2,1)}), bf16[2,16,16,1024]{3,2,0,1:T(8,128)(2,1)S(1)}, u32[]{:S(2)}, u32[]{:S(2)}) async-start(bf16[2,16,16,1024]{3,2,0,1:T(8,128)(2,1)} %copy.74), calls=%async_computation.3 | async-start | bytes 2097152 | tf_op jit(solution)/shard_map/all_to_all | solution.py:103
  78.6 1.6 copy.66
  80.2 14.4 %all-to-all-done.3 = bf16[2,16,16,1024]{3,2,0,1:T(8,128)(2,1)S(1)} async-done(((bf16[2,16,16,1024]{3,2,0,1:T(8,128)(2,1)}), bf16[2,16,16,1024]{3,2,0,1:T(8,128)(2,1)S(1)}, u32[]{:S(2)}, u32[]{:S(2)}) %all-to-all-start.3) | async-done | bytes 1048608 | tf_op jit(solution)/shard_map/all_to_all | solution.py:103
  95.6 3.7 %all-to-all-start.1 = ((bf16[2,16,16,1024]{3,2,0,1:T(8,128)(2,1)}), bf16[2,16,16,1024]{3,2,0,1:T(8,128)(2,1)S(1)}, u32[]{:S(2)}, u32[]{:S(2)}) async-start(bf16[2,16,16,1024]{3,2,0,1:T(8,128)(2,1)} %copy.66), calls=%async_computation.1 | async-start | bytes 2097152 | tf_op jit(solution)/shard_map/all_to_all | solution.py:100
  99.5 1.3 copy.75
  101.9 1.8 fusion.37
  103.7 1.9 convolution_subtract_fusion.1
  105.6 15.1 %all-to-all-done.1 = bf16[2,16,16,1024]{3,2,0,1:T(8,128)(2,1)S(1)} async-done(((bf16[2,16,16,1024]{3,2,0,1:T(8,128)(2,1)}), bf16[2,16,16,1024]{3,2,0,1:T(8,128)(2,1)S(1)}, u32[]{:S(2)}, u32[]{:S(2)}) %all-to-all-start.1) | async-done | bytes 1048608 | tf_op jit(solution)/shard_map/all_to_all | solution.py:100
  126.2 1.2 fusion.1
  127.5 1.2 fusion.5
  128.7 1.2 convolution_add_fusion
  130.0 1.6 subtract_bitcast_fusion
  131.6 1.5 pad_maximum_fusion
  133.0 4.2 %copy.84 = f32[2,2,128,1024]{3,1,0,2:T(2,128)} copy(f32[2,2,128,1024]{2,3,1,0:T(8,128)} %pad_maximum_fusion) | data formatting | bytes 4194304 | tf_op jit(solution)/shard_map/stack | solution.py:117
  137.2 50.2 %all_to_all.78 = f32[2,2,128,1024]{3,1,0,2:T(2,128)S(1)} all-to-all(f32[2,2,128,1024]{3,1,0,2:T(2,128)} %copy.84), channel_id=1, replica_groups=mesh['group'=2,'seq'=8,'chan'=2] {'seq'}, dimensions={2} | all-to-all | bytes 4194304 | tf_op jit(solution)/shard_map/all_to_all | solution.py:120
  187.4 1.2 copy.85
  190.6 1.7 squeeze.36
  192.3 2.0 fusion.71
  194.3 1.8 copy.87
  196.1 1.9 squeeze.37
  199.0 17.3 %all_to_all.79 = f32[8,16,1024]{2,1,0:T(8,128)S(1)} all-to-all(f32[8,16,1024]{2,1,0:T(8,128)S(1)} %copy.88), channel_id=1, replica_groups=mesh['group'=2,'seq'=8,'chan'=2] {'seq'}, dimensions={0} | all-to-all | bytes 1048576 | tf_op jit(solution)/shard_map/all_to_all | solution.py:124
  (63 shorter events, 17.1 us)
Async XLA Ops:
  0.0 9.6 %copy-start.9 = (s32[8,4]{0,1:T(4,128)S(1)}, s32[8,4]{0,1:T(4,128)}, u32[]{:S(2)}) copy-start(s32[8,4]{0,1:T(4,128)} %param.10) | copy-start | bytes 388
  0.0 9.7 %copy-start.7 = (bf16[1,8,1024]{2,1,0:T(8,128)(2,1)S(1)}, bf16[1,8,1024]{2,1,0:T(8,128)(2,1)}, u32[]{:S(2)}) copy-start(bf16[1,8,1024]{2,1,0:T(8,128)(2,1)} %param.8) | copy-start | bytes 49156
  0.0 46.9 %copy-start.5 = (bf16[128,3,1024]{2,0,1:T(8,128)(2,1)S(1)}, bf16[128,3,1024]{2,0,1:T(8,128)(2,1)}, u32[]{:S(2)}) copy-start(bf16[128,3,1024]{2,0,1:T(8,128)(2,1)} %param.7) | copy-start | bytes 2359300
  0.0 47.1 %copy-start.10 = (s32[8]{0:T(128)S(1)}, s32[8]{0:T(128)}, u32[]{:S(2)}) copy-start(s32[8]{0:T(128)} %param.9) | copy-start | bytes 100
  2.3 50.1 %all-to-all-start.2 = ((f32[1,128,1024]{2,0,1:T(1,128)}), f32[1,128,1024]{2,0,1:T(1,128)S(1)}, u32[]{:S(2)}, u32[]{:S(2)}) async-start(f32[1,128,1024]{2,0,1:T(1,128)} %broadcast_in_dim.12), calls=%async_computation.2 | async-start | bytes 1048576 | tf_op jit(solution)/shard_map/all_to_all | solution.py:97
  9.7 39.2 %copy-start.6 = (f32[3,3,1024]{2,1,0:T(4,128)S(1)}, f32[3,3,1024]{2,1,0:T(4,128)}, u32[]{:S(2)}) copy-start(f32[3,3,1024]{2,1,0:T(4,128)} %param.11) | copy-start | bytes 110596
  47.6 2.7 %collective-permute-start = (bf16[2,3,1024]{2,0,1:T(2,128)(2,1)S(1)}, bf16[2,3,1024]{2,0,1:T(2,128)(2,1)S(1)}, u32[]{:S(2)}, u32[]{:S(2)}) collective-permute-start(bf16[2,3,1024]{2,0,1:T(2,128)(2,1)S(1)} %fusion.58), channel_id=1, source_target_pairs={{0,2},{2,4},{4,6},{6,8},{8,10},{10,12},{12,14},{1,3},{3,5},{5,7},{... | collective-permute-start | bytes 36872 | tf_op jit(solution)/shard_map/ppermute | solution.py:14
  52.4 15.9 %all-to-all-start = ((f32[1,128,1024]{2,0,1:T(1,128)}), f32[1,128,1024]{2,0,1:T(1,128)S(1)}, u32[]{:S(2)}, u32[]{:S(2)}) async-start(f32[1,128,1024]{2,0,1:T(1,128)} %copy.63), calls=%async_computation | async-start | bytes 1048576 | tf_op jit(solution)/shard_map/all_to_all | solution.py:94
  68.4 1.3 copy-start.3
  73.8 20.9 %all-to-all-start.3 = ((bf16[2,16,16,1024]{3,2,0,1:T(8,128)(2,1)}), bf16[2,16,16,1024]{3,2,0,1:T(8,128)(2,1)S(1)}, u32[]{:S(2)}, u32[]{:S(2)}) async-start(bf16[2,16,16,1024]{3,2,0,1:T(8,128)(2,1)} %copy.74), calls=%async_computation.3 | async-start | bytes 2097152 | tf_op jit(solution)/shard_map/all_to_all | solution.py:103
  94.6 1.0 copy-start
  95.6 25.0 %all-to-all-start.1 = ((bf16[2,16,16,1024]{3,2,0,1:T(8,128)(2,1)}), bf16[2,16,16,1024]{3,2,0,1:T(8,128)(2,1)S(1)}, u32[]{:S(2)}, u32[]{:S(2)}) async-start(bf16[2,16,16,1024]{3,2,0,1:T(8,128)(2,1)} %copy.66), calls=%async_computation.1 | async-start | bytes 2097152 | tf_op jit(solution)/shard_map/all_to_all | solution.py:100
  122.7 1.2 copy-start.1
  123.9 1.2 copy-start.2
  192.3 2.0 copy-start.4
  198.7 17.6 %copy-start.8 = (f32[1024]{0:T(1024)S(1)}, f32[1024]{0:T(1024)}, u32[]{:S(2)}) copy-start(f32[1024]{0:T(1024)} %param.13) | copy-start | bytes 12292
where the time goes:
time: 218 us; the launch traced here: 217 us
  blocking collectives  105 us (48%)
  waiting for transfers between devices  37.5 us (17%)
  matrix products  24.5 us (11%)
  local copies, waits for them, and re-layouts  23.8 us (11%)
  starting transfers between devices  21.6 us (10%)
  other arithmetic  4.82 us (2%)
    all_to_all x1, blocking collectives, body(): lax.all_to_all(turned, 'seq', split_axis=2, concat_axis=1, tiled=True)  50.2 us
    all_gather x1, blocking collectives, body(): shards = lax.all_gather(library, 'seq', axis=0, tiled=True)  37.2 us
    dot_general x18, matrix products, exact_dot(): return jnp.einsum(pattern, matrix, tensor, precision=lax.Precision.HIGHEST)  24.2 us
    all_to_all x1, blocking collectives, body(): lax.all_to_all(positions, 'seq', split_axis=0, concat_axis=1, tiled=True)[0]  17.3 us
    all_to_all x1, waiting for transfers between devices, body(): lax.all_to_all(spread_signal.astype(jnp.bfloat16), 'seq', split_axis=1, c...  15.1 us
    all_to_all x1, waiting for transfers between devices, body(): lax.all_to_all(spread_taps.astype(jnp.bfloat16), 'seq', split_axis=1, con...  14.4 us
    all_to_all x1, starting transfers between devices, body(): lax.all_to_all(long_filter[None], 'seq', split_axis=1, concat_axis=0, til...  7.29 us
    all_to_all x1, waiting for transfers between devices, body(): lax.all_to_all(signal[None], 'seq', split_axis=1, concat_axis=0, tiled=True)  6.61 us
  transfers between devices with their start and end apart: 5, of which 4 were waited for; matrix products, arithmetic and copies ran while one was open for 7% of the time, Pallas kernels for 0%

commit v1 on v0

--- a/solution.py
+++ b/solution.py
@@ -90,9 +90,13 @@
         ].astype(jnp.float32)
     gating = shortened[:, 0]
     signal = shortened[:, 1] * shortened[:, 2]
-    spread_signal = to_modes(
-        lax.all_to_all(signal[None], "seq", split_axis=1, concat_axis=0, tiled=True)
+    numbers_finish = lambda xin: jnp.concatenate(
+        lax.all_to_all(
+            jnp.stack(jnp.split(xin, lax.axis_size("seq"), axis=1), axis=0), "seq", 0, 0
+        ),
+        axis=0,
     )
+    spread_signal = to_modes(numbers_finish(signal[None]))
     spread_taps = to_modes(
         lax.all_to_all(long_filter[None], "seq", split_axis=1, concat_axis=0, tiled=True)
     )

time: 218 us -> 208 us (0.954)
  blocking collectives: 105 us -> 79.5 us
  waiting for transfers between devices: 37.5 us -> 44.1 us
  local copies, waits for them, and re-layouts: 23.8 us -> 27.8 us
  starting transfers between devices: 21.6 us -> 24.2 us
    all_to_all x1, blocking collectives: 50.2 us -> 33.1 us  [body(): lax.all_to_all(turned, 'seq', split_axis=2, concat_axis=1, tiled=True)]
    all_to_all x1, waiting for transfers between devices: 14.4 us -> 21.1 us  [body(): lax.all_to_all(spread_taps.astype(jnp.bfloat16), 'seq', split_axis=1, con...]
    unnamed x25, local copies, waits for them, and re-layouts: 1.87 us -> 6.8 us
    all_to_all x1, waiting for transfers between devices: 0.01 us -> 4.91 us  [body(): lax.all_to_all(long_filter[None], 'seq', split_axis=1, concat_axis=0, til...]
    all_to_all x1, waiting for transfers between devices: 15.1 us -> 10.2 us  [body(): lax.all_to_all(spread_signal.astype(jnp.bfloat16), 'seq', split_axis=1, c...]
    all_gather x1, blocking collectives: 37.2 us -> 32.7 us  [body(): shards = lax.all_gather(library, 'seq', axis=0, tiled=True)]
    all_to_all x1, blocking collectives: 17.3 us -> 13.8 us  [body(): lax.all_to_all(positions, 'seq', split_axis=0, concat_axis=1, tiled=True)[0]]
    all_to_all x1, starting transfers between devices: 7.29 us -> 4.54 us  [body(): lax.all_to_all(long_filter[None], 'seq', split_axis=1, concat_axis=0, til...]
  transfers between devices with their start and end apart: 5 -> 5, of which waited for: 4 -> 4; matrix products, arithmetic and copies ran while one was open for 7% -> 9% of each run, Pallas kernels for 0% -> 0%
where the time goes in v1:
time: 208 us; the launch traced here: 207 us
  blocking collectives  79.5 us (38%)
  waiting for transfers between devices  44.1 us (21%)
  local copies, waits for them, and re-layouts  27.8 us (13%)
  matrix products  24.4 us (12%)
  starting transfers between devices  24.2 us (12%)
  other arithmetic  6.42 us (3%)
    all_to_all x1, blocking collectives, body(): lax.all_to_all(turned, 'seq', split_axis=2, concat_axis=1, tiled=True)  33.1 us
    all_gather x1, blocking collectives, body(): shards = lax.all_gather(library, 'seq', axis=0, tiled=True)  32.7 us
    dot_general x18, matrix products, exact_dot(): return jnp.einsum(pattern, matrix, tensor, precision=lax.Precision.HIGHEST)  24.2 us
    all_to_all x1, waiting for transfers between devices, body(): lax.all_to_all(spread_taps.astype(jnp.bfloat16), 'seq', split_axis=1, con...  21.1 us
    all_to_all x1, blocking collectives, body(): lax.all_to_all(positions, 'seq', split_axis=0, concat_axis=1, tiled=True)[0]  13.8 us
    all_to_all x1, waiting for transfers between devices, body(): lax.all_to_all(spread_signal.astype(jnp.bfloat16), 'seq', split_axis=1, c...  10.2 us
    all_to_all x1, waiting for transfers between devices, body(): lax.all_to_all(jnp.stack(jnp.split(xin, lax.axis_size('seq'), axis=1), ax...  7.84 us
    all_to_all x1, starting transfers between devices, body(): lax.all_to_all(jnp.stack(jnp.split(xin, lax.axis_size('seq'), axis=1), ax...  7.18 us
  transfers between devices with their start and end apart: 5, of which 4 were waited for; matrix products, arithmetic and copies ran while one was open for 9% of the time, Pallas kernels for 0%

profile of v1, /device:TPU:0, one launch (start us, length us, event | category | flops | bytes accessed | tf_op | source)
XLA Modules:
  0.0 206.8 jit_solution(16063340886157073671)
XLA Ops:
  0.8 32.7 %all_gather.3 = bf16[8,8,1024]{2,1,0:T(8,128)(2,1)S(1)} all-gather(bf16[1,8,1024]{2,1,0:T(8,128)(2,1)} %param.8), channel_id=1, replica_groups=mesh['group'=2,'seq'=8,'chan'=2] {'seq'}, dimensions={0}, use_global_device_ids=true | all-gather | bytes 147456 | tf_op jit(solution)/shard_map/all_gather | solution.py:75
  36.8 3.4 %collective-permute-start = (bf16[2,3,1024]{2,0,1:T(2,128)(2,1)S(1)}, bf16[2,3,1024]{2,0,1:T(2,128)(2,1)S(1)}, u32[]{:S(2)}, u32[]{:S(2)}) collective-permute-start(bf16[2,3,1024]{2,0,1:T(2,128)(2,1)S(1)} %fusion.68), channel_id=1, source_target_pairs={{0,2},{2,4},{4,6},{6,8},{8,10},{10,12},{12,14},{1,3},{3,5},{5,7},{... | collective-permute-start | bytes 36872 | tf_op jit(solution)/shard_map/ppermute | solution.py:14
  41.4 4.5 %all-to-all-start.2 = ((f32[1,128,1024]{2,0,1:T(1,128)}), f32[1,128,1024]{2,0,1:T(1,128)S(1)}, u32[]{:S(2)}, u32[]{:S(2)}) async-start(f32[1,128,1024]{2,0,1:T(1,128)} %broadcast_in_dim.12), calls=%async_computation.2 | async-start | bytes 1048576 | tf_op jit(solution)/shard_map/all_to_all | solution.py:101
  51.7 4.9 %all-to-all-done.2 = f32[1,128,1024]{2,0,1:T(1,128)S(1)} async-done(((f32[1,128,1024]{2,0,1:T(1,128)}), f32[1,128,1024]{2,0,1:T(1,128)S(1)}, u32[]{:S(2)}, u32[]{:S(2)}) %all-to-all-start.2) | async-done | bytes 524320 | tf_op jit(solution)/shard_map/all_to_all | solution.py:101
  56.6 7.2 %all-to-all-start = ((f32[8,1,16,1024]{3,2,1,0:T(8,128)}), f32[8,1,16,1024]{3,2,1,0:T(8,128)S(1)}, u32[]{:S(2)}, u32[]{:S(2)}) async-start(f32[8,1,16,1024]{3,2,1,0:T(8,128)} %fusion.27), calls=%async_computation | async-start | bytes 1048576 | tf_op jit(solution)/shard_map/all_to_all | solution.py:94
  64.1 2.2 %convolution_negate_fusion = f32[16,16,1024]{2,0,1:T(8,128)} fusion(f32[8,16,1024]{2,1,0:T(8,128)S(1)} %bitcast.173), kind=kOutput, calls=%fused_computation.2 | convolution fusion | flops 25429760 | bytes 1572864 | tf_op jit(solution)/shard_map/kq,qgc->kgc/dot_general | solution.py:18
  66.3 7.8 %all-to-all-done = f32[8,1,16,1024]{3,2,1,0:T(8,128)S(1)} async-done(((f32[8,1,16,1024]{3,2,1,0:T(8,128)}), f32[8,1,16,1024]{3,2,1,0:T(8,128)S(1)}, u32[]{:S(2)}, u32[]{:S(2)}) %all-to-all-start) | async-done | bytes 524320 | tf_op jit(solution)/shard_map/all_to_all | solution.py:94
  74.1 1.2 convolution_negate_fusion.1
  75.3 1.2 fusion.15
  76.5 2.4 %fusion.9 = (bf16[1,16,16,1024]{3,1,2,0:T(8,128)(2,1)S(1)}, bf16[1,16,16,1024]{3,1,2,0:T(8,128)(2,1)S(1)}, bf16[1,16,16,1024]{3,1,2,0:T(8,128)(2,1)S(1)}, bf16[1,16,16,1024]{3,1,2,0:T(8,128)(2,1)}) fusion(f32[16,16,1024]{2,0,1:T(8,128)S(1)} %copy-done.3, f32[16,16]{0,1:T(8,128)S(1)} %get-tuple-element.27, f32[16,16]{0,1:T(8,128)S(1)} %get-tuple-element.26, ...), kind=kOutput, calls=%fused_computation.35 | convolution fusion | flops 29361920 | bytes 5769216 | tf_op jit(solution)/shard_map/kq,qgc->kgc/dot_general | solution.py:18
  79.1 1.5 copy.73
  80.6 3.7 %all-to-all-start.3 = ((bf16[2,16,16,1024]{3,2,0,1:T(8,128)(2,1)}), bf16[2,16,16,1024]{3,2,0,1:T(8,128)(2,1)S(1)}, u32[]{:S(2)}, u32[]{:S(2)}) async-start(bf16[2,16,16,1024]{3,2,0,1:T(8,128)(2,1)} %copy.73), calls=%async_computation.3 | async-start | bytes 2097152 | tf_op jit(solution)/shard_map/all_to_all | solution.py:107
  85.5 1.6 copy.65
  87.0 21.1 %all-to-all-done.3 = bf16[2,16,16,1024]{3,2,0,1:T(8,128)(2,1)S(1)} async-done(((bf16[2,16,16,1024]{3,2,0,1:T(8,128)(2,1)}), bf16[2,16,16,1024]{3,2,0,1:T(8,128)(2,1)S(1)}, u32[]{:S(2)}, u32[]{:S(2)}) %all-to-all-start.3) | async-done | bytes 1048608 | tf_op jit(solution)/shard_map/all_to_all | solution.py:107
  109.1 5.4 %all-to-all-start.1 = ((bf16[2,16,16,1024]{3,2,0,1:T(8,128)(2,1)}), bf16[2,16,16,1024]{3,2,0,1:T(8,128)(2,1)S(1)}, u32[]{:S(2)}, u32[]{:S(2)}) async-start(bf16[2,16,16,1024]{3,2,0,1:T(8,128)(2,1)} %copy.65), calls=%async_computation.1 | async-start | bytes 2097152 | tf_op jit(solution)/shard_map/all_to_all | solution.py:104
  114.7 1.3 copy.74
  117.1 1.8 fusion.47
  118.9 1.9 convolution_subtract_fusion.1
  120.7 10.2 %all-to-all-done.1 = bf16[2,16,16,1024]{3,2,0,1:T(8,128)(2,1)S(1)} async-done(((bf16[2,16,16,1024]{3,2,0,1:T(8,128)(2,1)}), bf16[2,16,16,1024]{3,2,0,1:T(8,128)(2,1)S(1)}, u32[]{:S(2)}, u32[]{:S(2)}) %all-to-all-start.1) | async-done | bytes 1048608 | tf_op jit(solution)/shard_map/all_to_all | solution.py:104
  136.5 1.2 fusion.1
  137.8 1.2 fusion.5
  139.0 1.2 convolution_add_fusion
  140.3 1.6 subtract_bitcast_fusion
  141.9 1.5 pad_maximum_fusion
  143.3 4.2 %copy.83 = f32[2,2,128,1024]{3,1,0,2:T(2,128)} copy(f32[2,2,128,1024]{2,3,1,0:T(8,128)} %pad_maximum_fusion) | data formatting | bytes 4194304 | tf_op jit(solution)/shard_map/stack | solution.py:121
  147.5 33.1 %all_to_all.71 = f32[2,2,128,1024]{3,1,0,2:T(2,128)S(1)} all-to-all(f32[2,2,128,1024]{3,1,0,2:T(2,128)} %copy.83), channel_id=1, replica_groups=mesh['group'=2,'seq'=8,'chan'=2] {'seq'}, dimensions={2} | all-to-all | bytes 4194304 | tf_op jit(solution)/shard_map/all_to_all | solution.py:124
  180.6 1.2 copy.84
  183.8 1.7 squeeze.36
  185.5 2.0 fusion.81
  187.4 1.8 copy.86
  189.2 1.9 squeeze.37
  192.2 13.8 %all_to_all.72 = f32[8,16,1024]{2,1,0:T(8,128)S(1)} all-to-all(f32[8,16,1024]{2,1,0:T(8,128)S(1)} %copy.87), channel_id=1, replica_groups=mesh['group'=2,'seq'=8,'chan'=2] {'seq'}, dimensions={0} | all-to-all | bytes 1048576 | tf_op jit(solution)/shard_map/all_to_all | solution.py:128
  (63 shorter events, 24.0 us)
Async XLA Ops:
  0.8 39.4 %copy-start.5 = (f32[128,1024]{1,0:T(8,128)S(1)}, f32[128,1024]{1,0:T(8,128)}, u32[]{:S(2)}) copy-start(f32[128,1024]{1,0:T(8,128)} %param.12) | copy-start | bytes 1572868
  36.8 9.2 %copy-start.6 = (f32[3,3,1024]{2,1,0:T(4,128)S(1)}, f32[3,3,1024]{2,1,0:T(4,128)}, u32[]{:S(2)}) copy-start(f32[3,3,1024]{2,1,0:T(4,128)} %param.11) | copy-start | bytes 110596
  36.8 9.1 %collective-permute-start = (bf16[2,3,1024]{2,0,1:T(2,128)(2,1)S(1)}, bf16[2,3,1024]{2,0,1:T(2,128)(2,1)S(1)}, u32[]{:S(2)}, u32[]{:S(2)}) collective-permute-start(bf16[2,3,1024]{2,0,1:T(2,128)(2,1)S(1)} %fusion.68), channel_id=1, source_target_pairs={{0,2},{2,4},{4,6},{6,8},{8,10},{10,12},{12,14},{1,3},{3,5},{5,7},{... | collective-permute-start | bytes 36872 | tf_op jit(solution)/shard_map/ppermute | solution.py:14
  41.4 15.2 %all-to-all-start.2 = ((f32[1,128,1024]{2,0,1:T(1,128)}), f32[1,128,1024]{2,0,1:T(1,128)S(1)}, u32[]{:S(2)}, u32[]{:S(2)}) async-start(f32[1,128,1024]{2,0,1:T(1,128)} %broadcast_in_dim.12), calls=%async_computation.2 | async-start | bytes 1048576 | tf_op jit(solution)/shard_map/all_to_all | solution.py:101
  56.6 17.5 %all-to-all-start = ((f32[8,1,16,1024]{3,2,1,0:T(8,128)}), f32[8,1,16,1024]{3,2,1,0:T(8,128)S(1)}, u32[]{:S(2)}, u32[]{:S(2)}) async-start(f32[8,1,16,1024]{3,2,1,0:T(8,128)} %fusion.27), calls=%async_computation | async-start | bytes 1048576 | tf_op jit(solution)/shard_map/all_to_all | solution.py:94
  74.1 2.4 %copy-start.3 = (f32[16,16,1024]{2,0,1:T(8,128)S(1)}, f32[16,16,1024]{2,0,1:T(8,128)}, u32[]{:S(2)}) copy-start(f32[16,16,1024]{2,0,1:T(8,128)} %convolution_negate_fusion) | copy-start | bytes 3145732
  80.6 27.5 %all-to-all-start.3 = ((bf16[2,16,16,1024]{3,2,0,1:T(8,128)(2,1)}), bf16[2,16,16,1024]{3,2,0,1:T(8,128)(2,1)S(1)}, u32[]{:S(2)}, u32[]{:S(2)}) async-start(bf16[2,16,16,1024]{3,2,0,1:T(8,128)(2,1)} %copy.73), calls=%async_computation.3 | async-start | bytes 2097152 | tf_op jit(solution)/shard_map/all_to_all | solution.py:107
  108.2 1.0 copy-start
  109.1 21.8 %all-to-all-start.1 = ((bf16[2,16,16,1024]{3,2,0,1:T(8,128)(2,1)}), bf16[2,16,16,1024]{3,2,0,1:T(8,128)(2,1)S(1)}, u32[]{:S(2)}, u32[]{:S(2)}) async-start(bf16[2,16,16,1024]{3,2,0,1:T(8,128)(2,1)} %copy.65), calls=%async_computation.1 | async-start | bytes 2097152 | tf_op jit(solution)/shard_map/all_to_all | solution.py:104
  133.0 1.2 copy-start.1
  134.2 1.2 copy-start.2
  185.5 2.0 copy-start.4
  191.8 14.1 %copy-start.7 = (f32[1024]{0:T(1024)S(1)}, f32[1024]{0:T(1024)}, u32[]{:S(2)}) copy-start(f32[1024]{0:T(1024)} %param.13) | copy-start | bytes 12292
